TPU v7x, 32 devices: a whole 2x2x4 slice. The times are simulated.
32 devices in a mesh: groups: 2 (over y), lon: 4 (over z), chan: 2 (over x), lat: 2 (over core).
Axes of the slice: x: 2, y: 2, z: 4, core: 2. Of those that a mesh axis runs over, the one named last changes fastest.
Arguments:
- inputs: bfloat16 [256, 64, 512], P('chan', ('groups', 'lat'), 'lon'), parts along dimension 1, may hold values from -6 to 6
- cotangent: bfloat16 [256, 64, 512], P('chan', ('groups', 'lat'), 'lon'), parts along dimension 1, may hold values from -6 to 6
- weight: bfloat16 [3, 3, 256, 256], P(None, None, 'chan'), may hold values from -0.125 to 0.125
- bias_vector: float32 [256], P('chan'), may hold values from -4 to 4
Outputs:
- input_grad: bfloat16 [256, 64, 512], P('chan', ('groups', 'lat'), 'lon'), parts along dimension 1
- weight_grad: float32 [6, 3, 256, 256], P('groups', None, 'chan'), parts along dimension 0
- bias_grad: float32 [512], P(('groups', 'chan')), parts along dimension 0
There are 2 independent parts, one for each index of `groups`. A program takes and returns all parts, laid end to end along the dimension named above; an argument that names none is the same for every part. Nothing has to cross between parts.
All inputs are finite; a program needn't handle non-finite values.
Results may differ from a plain program's by a relative error of at most 0.007.
Values may be sent and summed in bfloat16 or wider, within the bound.
No kernel may reach another device: no remote copies, remote signals or barrier semaphores. Data moves between devices by JAX's collectives and lax.ppermute only.
A program may use at most 64 MiB of HBM per device.

v0:
```python
import jax
import jax.numpy as jnp
from jax import lax
from jax.sharding import PartitionSpec as P


def padded_2(shard, sides, width):
    for axis, dim in sides:
        devices, length = (lax.axis_size(axis), shard.shape[dim])
        up = [(i, (i + 1) % devices) for i in range(devices)]
        down = [(j, i) for i, j in up]
        last = lax.slice_in_dim(shard, length - width, length, axis=dim)
        initial = lax.slice_in_dim(shard, 0, width, axis=dim)
        before = lax.ppermute(last, axis, up)
        after = lax.ppermute(initial, axis, down)
        shard = jnp.concatenate([before, shard, after], axis=dim)
    return shard


def gelu_slope(preact):
    normal_cdf = 0.5 * (1.0 + jax.scipy.special.erf(preact * 0.7071067811865476))
    density = jnp.exp(-0.5 * preact * preact) * 0.3989422804014327
    return normal_cdf + preact * density


def mask_rims(padded):
    lat_index = lax.axis_index("lat")
    band_count = lax.axis_size("lat")
    row_ids = jnp.arange(padded.shape[1])
    outside = (row_ids == 0) & (lat_index == 0) | (row_ids == padded.shape[1] - 1) & (
        lat_index == band_count - 1
    )
    return jnp.where(outside[None, :, None], jnp.zeros((), padded.dtype), padded)


def window_of(field, first_row, first_col, row_count, column_count):
    return field[
        :, first_row : first_row + row_count, first_col : first_col + column_count
    ].reshape(field.shape[0], -1)


def local(inputs, cotangent, weight, bias_vector):
    own_channels, row_count, column_count = inputs.shape
    input_pad = mask_rims(padded_2(inputs, (("lon", 2), ("lat", 1)), 1))
    input_all = lax.all_gather(input_pad, "chan", axis=0, tiled=True)
    preact = jnp.zeros((own_channels, row_count * column_count), jnp.float32)
    for tap_row in range(3):
        for tap_col in range(3):
            window = window_of(input_all, tap_row, tap_col, row_count, column_count)
            preact = preact + jnp.dot(
                weight[tap_row, tap_col], window, preferred_element_type=jnp.float32
            )
    preact = preact + bias_vector[:, None]
    upstream = cotangent.reshape(own_channels, -1).astype(jnp.float32)
    grad_pre = (upstream * gelu_slope(preact)).astype(jnp.bfloat16)
    bias_part = jnp.sum(grad_pre.astype(jnp.float32), axis=1)
    taps = []
    for tap_row in range(3):
        row_taps = []
        for tap_col in range(3):
            window = window_of(input_all, tap_row, tap_col, row_count, column_count)
            row_taps.append(
                lax.dot_general(
                    grad_pre, window, (((1,), (1,)), ((), ())), preferred_element_type=jnp.float32
                )
            )
        taps.append(jnp.stack(row_taps))
    weight_part = jnp.stack(taps)
    weight_grad, bias_grad = lax.psum((weight_part, bias_part), ("lon", "lat"))
    grad_field = grad_pre.reshape(own_channels, row_count, column_count)
    grad_pad = mask_rims(padded_2(grad_field, (("lon", 2), ("lat", 1)), 1))
    amount = lax.axis_size("chan") * own_channels
    summed = jnp.zeros((amount, row_count * column_count), jnp.float32)
    for tap_row in range(3):
        for tap_col in range(3):
            kernel_cols = weight[tap_row, tap_col]
            window = window_of(grad_pad, 2 - tap_row, 2 - tap_col, row_count, column_count)
            summed = summed + lax.dot_general(
                kernel_cols, window, (((0,), (0,)), ((), ())), preferred_element_type=jnp.float32
            )
    input_sum = lax.psum_scatter(
        summed.reshape(amount, row_count, column_count), "chan", scatter_dimension=0, tiled=True
    )
    return (input_sum.astype(jnp.bfloat16), weight_grad, bias_grad)


def solution(mesh):
    placed = (
        P("chan", ("groups", "lat"), "lon"),
        P("chan", ("groups", "lat"), "lon"),
        P(None, None, "chan", None),
        P("chan"),
    )
    return jax.shard_map(
        local,
        mesh=mesh,
        in_specs=placed,
        out_specs=(
            P("chan", ("groups", "lat"), "lon"),
            P("groups", None, "chan", None),
            P(("groups", "chan")),
        ),
        check_vma=False,
    )
```

profile of v0, /device:TPU:0, one launch (start us, length us, event | category | flops | bytes accessed | tf_op | source)
XLA Modules:
  0.0 177.4 jit_solution(9235394544272731963)
XLA Ops:
  7.2 1.5 copy.13
  8.8 3.1 %collective-permute-start = (bf16[128,16,1]{0,2,1:T(2,128)(2,1)S(1)}, bf16[128,16,1]{0,2,1:T(2,128)(2,1)S(1)}, u32[]{:S(2)}, u32[]{:S(2)}) collective-permute-start(bf16[128,16,1]{0,2,1:T(2,128)(2,1)S(1)} %get-tuple-element.27), channel_id=1, source_target_pairs={{0,4},{4,8},{8,12},{12,0},{1,5},{5,9},{9,13},{13,1},{2,6},{6,10},{... | collective-permute-start | bytes 12296 | tf_op jit(solution)/shard_map/ppermute | solution.py:14
  11.8 2.1 %collective-permute-start.1 = (bf16[128,16,1]{0,2,1:T(2,128)(2,1)S(1)}, bf16[128,16,1]{0,2,1:T(2,128)(2,1)S(1)}, u32[]{:S(2)}, u32[]{:S(2)}) collective-permute-start(bf16[128,16,1]{0,2,1:T(2,128)(2,1)S(1)} %get-tuple-element.28), channel_id=1, source_target_pairs={{4,0},{8,4},{12,8},{0,12},{5,1},{9,5},{13,9},{1,13},{6,2},{10,6},{... | collective-permute-start | bytes 12296 | tf_op jit(solution)/shard_map/ppermute | solution.py:15
  13.9 1.6 collective-permute-done
  17.0 1.1 maximum_select_fusion
  18.2 1.4 copy.12
  19.6 23.9 %all-gather.2.cloned.1.call-done = bf16[256,18,130]{0,2,1:T(8,128)(2,1)} async-done(((bf16[128,18,130]{0,2,1:T(8,128)(2,1)}), bf16[256,18,130]{0,2,1:T(8,128)(2,1)}) %all-gather.2.cloned.1.call-update) | async-done | bytes 1198096 | tf_op jit(solution)/shard_map/all_gather | solution.py:45
  43.5 8.3 %fusion.46 = (bf16[256,16,128]{0,2,1:T(8,128)(2,1)S(1)}, bf16[256,16,128]{0,2,1:T(8,128)(2,1)S(1)}, bf16[256,16,128]{0,2,1:T(8,128)(2,1)S(1)}, bf16[256,16,128]{...) fusion(bf16[256,18,130]{0,2,1:T(8,128)(2,1)} %all-gather.2.clon, ...), kind=kLoop, calls=%fused_computation.86 | loop fusion | bytes 18874368 | tf_op jit(solution)/shard_map/slice | solution.py:37
  55.6 0.7 copy-done.13
  56.3 0.7 convert_reduce_fusion
  57.1 1.5 collective-permute-start.4
  58.6 2.3 %collective-permute-start.5 = (bf16[128,16,1]{0,2,1:T(2,128)(2,1)S(1)}, bf16[128,16,1]{0,2,1:T(2,128)(2,1)S(1)}, u32[]{:S(2)}, u32[]{:S(2)}) collective-permute-start(bf16[128,16,1]{0,2,1:T(2,128)(2,1)S(1)} %get-tuple-element.26), channel_id=1, source_target_pairs={{4,0},{8,4},{12,8},{0,12},{5,1},{9,5},{13,9},{1,13},{6,2},{10,6},{... | collective-permute-start | bytes 12296 | tf_op jit(solution)/shard_map/ppermute | solution.py:15
  60.9 1.6 collective-permute-done.4
  64.4 0.9 fusion.47
  68.6 1.7 convolution_add_fusion
  70.4 3.0 %copy.16 = f32[256,16,128]{2,1,0:T(8,128)} copy(f32[256,16,128]{0,2,1:T(8,128)} %bitcast.154) | data formatting | bytes 4194304 | tf_op jit(solution)/shard_map/reshape | solution.py:82
  73.6 1.7 convolution_bitcast_fusion
  75.3 1.7 convolution_bitcast_fusion.1
  80.6 1.1 pad_maximum_fusion
  81.8 17.9 %psum.15 = f32[128]{0:T(128)} all-reduce(f32[128]{0:T(128)S(1)} %get-tuple-element.29), channel_id=1, replica_groups=mesh['groups'=2,'lon'=4,'chan'=2,'lat'=2] {'lon','lat'}, use_global_device_ids=true, to_apply=%region_3.4 | all-reduce | flops 128 | bytes 1024 | tf_op jit(solution)/shard_map/psum | solution.py:69
  99.6 6.3 %reduce-scatter.2.cloned.1.call-done = f32[128,16,128]{2,1,0:T(8,128)} async-done(((f32[256,16,128]{2,1,0:T(8,128)}), f32[128,16,128]{2,1,0:T(8,128)}) %reduce-scatter.2.cloned.1.call-update) | async-done | bytes 1048592 | tf_op jit(solution)/shard_map/reduce_scatter | solution.py:81
  105.9 2.1 %convert_element_type.18 = bf16[128,16,128]{2,1,0:T(8,128)(2,1)} convert(f32[128,16,128]{2,1,0:T(8,128)} %reduce-scatter.2.cloned.1.call-done) | non-fusion elementwise | flops 262144 | bytes 1572864 | tf_op jit(solution)/shard_map/convert_element_type | solution.py:84
  108.0 60.5 %all-reduce.2.cloned.1.call-done = f32[3,3,128,256]{3,2,1,0:T(8,128)} async-done(((f32[3,3,128,256]{3,2,1,0:T(8,128)}), f32[3,3,128,256]{3,2,1,0:T(8,128)}) %all-reduce.2.cloned.1.call-update) | async-done | bytes 1179664 | tf_op jit(solution)/shard_map/psum | solution.py:69
  168.5 2.4 %copy.18 = f32[3,3,128,256]{3,2,1,0:T(8,128)} copy(f32[3,3,128,256]{3,2,1,0:T(8,128)} %all-reduce.2.cloned.1.call-done) | data formatting | bytes 2359296
  (78 shorter events, 14.1 us)
Async XLA Ops:
  7.2 11.1 %copy-start.14 = (bf16[128,16,128]{2,1,0:T(8,128)(2,1)S(1)}, bf16[128,16,128]{2,1,0:T(8,128)(2,1)}, u32[]{:S(2)}) copy-start(bf16[128,16,128]{2,1,0:T(8,128)(2,1)} %param.5) | copy-start | bytes 1572868
  7.2 36.3 %all-gather.2.cloned.1.call-start = ((), (), s32[]{:S(2)}) async-start(), calls=%async_computation.1 | async-start | bytes 1880064 | tf_op jit(solution)/shard_map/all_gather | solution.py:45
  8.8 6.8 %collective-permute-start = (bf16[128,16,1]{0,2,1:T(2,128)(2,1)S(1)}, bf16[128,16,1]{0,2,1:T(2,128)(2,1)S(1)}, u32[]{:S(2)}, u32[]{:S(2)}) collective-permute-start(bf16[128,16,1]{0,2,1:T(2,128)(2,1)S(1)} %get-tuple-element.27), channel_id=1, source_target_pairs={{0,4},{4,8},{8,12},{12,0},{1,5},{5,9},{9,13},{13,1},{2,6},{6,10},{... | collective-permute-start | bytes 12296 | tf_op jit(solution)/shard_map/ppermute | solution.py:14
  11.8 3.7 %collective-permute-start.1 = (bf16[128,16,1]{0,2,1:T(2,128)(2,1)S(1)}, bf16[128,16,1]{0,2,1:T(2,128)(2,1)S(1)}, u32[]{:S(2)}, u32[]{:S(2)}) collective-permute-start(bf16[128,16,1]{0,2,1:T(2,128)(2,1)S(1)} %get-tuple-element.28), channel_id=1, source_target_pairs={{4,0},{8,4},{12,8},{0,12},{5,1},{9,5},{13,9},{1,13},{6,2},{10,6},{... | collective-permute-start | bytes 12296 | tf_op jit(solution)/shard_map/ppermute | solution.py:15
  15.6 1.3 collective-permute-start.2
  15.7 1.4 collective-permute-start.3
  18.2 87.8 %reduce-scatter.2.cloned.1.call-start = ((), (), s32[]{:S(2)}) async-start(), calls=%async_computation.2 | async-start | bytes 3145728 | tf_op jit(solution)/shard_map/reduce_scatter | solution.py:81
  19.6 32.3 %copy-start.12 = (bf16[3,3,128,256]{3,2,1,0:T(8,128)(2,1)S(1)}, bf16[3,3,128,256]{3,2,1,0:T(8,128)(2,1)}, u32[]{:S(2)}) copy-start(bf16[3,3,128,256]{3,2,1,0:T(8,128)(2,1)} %param.6) | copy-start | bytes 1769476
  51.9 1.4 copy-start.2
  51.9 1.9 %copy-start.4 = (bf16[256,16,128]{0,2,1:T(8,128)(2,1)}, bf16[256,16,128]{0,2,1:T(8,128)(2,1)S(1)}, u32[]{:S(2)}) copy-start(bf16[256,16,128]{0,2,1:T(8,128)(2,1)S(1)} %get-tuple-element.7) | copy-start | bytes 3145732
  51.9 2.3 %copy-start.6 = (bf16[256,16,128]{0,2,1:T(8,128)(2,1)}, bf16[256,16,128]{0,2,1:T(8,128)(2,1)S(1)}, u32[]{:S(2)}) copy-start(bf16[256,16,128]{0,2,1:T(8,128)(2,1)S(1)} %get-tuple-element.6) | copy-start | bytes 3145732
  51.9 2.7 %copy-start.8 = (bf16[256,16,128]{0,2,1:T(8,128)(2,1)}, bf16[256,16,128]{0,2,1:T(8,128)(2,1)S(1)}, u32[]{:S(2)}) copy-start(bf16[256,16,128]{0,2,1:T(8,128)(2,1)S(1)} %get-tuple-element.5) | copy-start | bytes 3145732
  51.9 3.2 %copy-start.10 = (bf16[256,16,128]{0,2,1:T(8,128)(2,1)}, bf16[256,16,128]{0,2,1:T(8,128)(2,1)S(1)}, u32[]{:S(2)}) copy-start(bf16[256,16,128]{0,2,1:T(8,128)(2,1)S(1)} %get-tuple-element.4) | copy-start | bytes 3145732
  51.9 3.6 %copy-start.11 = (bf16[256,16,128]{0,2,1:T(8,128)(2,1)}, bf16[256,16,128]{0,2,1:T(8,128)(2,1)S(1)}, u32[]{:S(2)}) copy-start(bf16[256,16,128]{0,2,1:T(8,128)(2,1)S(1)} %get-tuple-element.3) | copy-start | bytes 3145732
  55.1 1.2 copy-start.13
  57.1 5.5 %collective-permute-start.4 = (bf16[128,16,1]{0,2,1:T(2,128)(2,1)S(1)}, bf16[128,16,1]{0,2,1:T(2,128)(2,1)S(1)}, u32[]{:S(2)}, u32[]{:S(2)}) collective-permute-start(bf16[128,16,1]{0,2,1:T(2,128)(2,1)S(1)} %get-tuple-element.25), channel_id=1, source_target_pairs={{0,4},{4,8},{8,12},{12,0},{1,5},{5,9},{9,13},{13,1},{2,6},{6,10},{... | collective-permute-start | bytes 12296 | tf_op jit(solution)/shard_map/ppermute | solution.py:14
  58.6 4.0 %collective-permute-start.5 = (bf16[128,16,1]{0,2,1:T(2,128)(2,1)S(1)}, bf16[128,16,1]{0,2,1:T(2,128)(2,1)S(1)}, u32[]{:S(2)}, u32[]{:S(2)}) collective-permute-start(bf16[128,16,1]{0,2,1:T(2,128)(2,1)S(1)} %get-tuple-element.26), channel_id=1, source_target_pairs={{4,0},{8,4},{12,8},{0,12},{5,1},{9,5},{13,9},{1,13},{6,2},{10,6},{... | collective-permute-start | bytes 12296 | tf_op jit(solution)/shard_map/ppermute | solution.py:15
  62.6 1.3 collective-permute-start.6
  62.7 1.4 collective-permute-start.7
  73.4 95.1 %all-reduce.2.cloned.1.call-start = ((), (), s32[]{:S(2)}) async-start(), calls=%async_computation.3 | async-start | bytes 2359296 | tf_op jit(solution)/shard_map/psum | solution.py:69
  73.6 3.3 %copy-start.9 = (bf16[256,16,128]{0,2,1:T(8,128)(2,1)S(1)}, bf16[256,16,128]{0,2,1:T(8,128)(2,1)}, u32[]{:S(2)}) copy-start(bf16[256,16,128]{0,2,1:T(8,128)(2,1)} %copy-done.8) | copy-start | bytes 3145732
  75.3 2.1 %copy-start.7 = (bf16[256,16,128]{0,2,1:T(8,128)(2,1)S(1)}, bf16[256,16,128]{0,2,1:T(8,128)(2,1)}, u32[]{:S(2)}) copy-start(bf16[256,16,128]{0,2,1:T(8,128)(2,1)} %copy-done.6) | copy-start | bytes 3145732
  77.4 1.3 copy-start.3
  78.2 1.3 copy-start.1
  (3 other events, 3.5 us)
Sparse Core Ops, SparseCore 0:
  18.3 25.1 all-gather.1
  73.5 32.3 reduce-scatter.1
  109.0 59.5 all-reduce.1
where the time goes:
time: 178 us; the launch traced here: 177 us
  waiting for transfers between devices  95.8 us (54%)
  local copies, waits for them, and re-layouts  19.5 us (11%)
  blocking collectives  17.9 us (10%)
  matrix products  15 us (8%)
  between operations  14.2 us (8%)
  starting transfers between devices  10.5 us (6%)
  other arithmetic  4.73 us (3%)
    psum x1, waiting for transfers between devices, local(): weight_grad, bias_grad = lax.psum((weight_part, bias_part), ('lon', 'lat'))  60.5 us
    all_gather x1, waiting for transfers between devices, local(): input_all = lax.all_gather(input_pad, 'chan', axis=0, tiled=True)  23.9 us
    psum x1, blocking collectives, local(): weight_grad, bias_grad = lax.psum((weight_part, bias_part), ('lon', 'lat'))  17.9 us
    slice x2, local copies, waits for them, and re-layouts, window_of(): field[:, first_row:first_row + row_count, first_col:first_col + column_co...  9.24 us
    reduce_scatter x1, waiting for transfers between devices, local(): lax.psum_scatter(summed.reshape(amount, row_count, column_count), 'chan',...  6.31 us
    unnamed x34, local copies, waits for them, and re-layouts  5.76 us
    dot_general x9, matrix products, local(): lax.dot_general(grad_pre, window, (((1,), (1,)), ((), ())), preferred_ele...  5.76 us
    ppermute x4, starting transfers between devices, padded_2(): after = lax.ppermute(initial, axis, down)  5.42 us
  transfers between devices with their start and end apart: 11, of which 9 were waited for; matrix products, arithmetic and copies ran while one was open for 6% of the time, Pallas kernels for 0%

commit v1 on v0

--- a/solution.py
+++ b/solution.py
@@ -2,6 +2,18 @@
 import jax.numpy as jnp
 from jax import lax
 from jax.sharding import PartitionSpec as P
+
+
+def doubled_up(value, axis, dim):
+    ways, here, turn = (lax.axis_size(axis), lax.axis_index(axis), value.shape[dim])
+    line, have = (value, 1)
+    while have < ways:
+        line = jnp.concatenate(
+            [line, lax.ppermute(line, axis, [(d, (d - have) % ways) for d in range(ways)])],
+            axis=dim,
+        )
+        have = 2 * have
+    return jnp.roll(line, here * turn, axis=dim)
 
 
 def padded_2(shard, sides, width):
@@ -42,7 +54,7 @@
 def local(inputs, cotangent, weight, bias_vector):
     own_channels, row_count, column_count = inputs.shape
     input_pad = mask_rims(padded_2(inputs, (("lon", 2), ("lat", 1)), 1))
-    input_all = lax.all_gather(input_pad, "chan", axis=0, tiled=True)
+    input_all = doubled_up(input_pad, "chan", 0)
     preact = jnp.zeros((own_channels, row_count * column_count), jnp.float32)
     for tap_row in range(3):
         for tap_col in range(3):

time: 178 us -> 140 us (0.79)
  waiting for transfers between devices: 95.8 us -> 59.4 us
  local copies, waits for them, and re-layouts: 19.5 us -> 13.6 us
    psum x1, waiting for transfers between devices: 60.5 us -> 34 us  [local(): weight_grad, bias_grad = lax.psum((weight_part, bias_part), ('lon', 'lat'))]
    all_gather x1 -> x0, waiting for transfers between devices: 23.9 us -> none  [local(): input_all = lax.all_gather(input_pad, 'chan', axis=0, tiled=True)]
    ppermute x0 -> x1, waiting for transfers between devices: none -> 13.3 us  [doubled_up(): lax.ppermute(line, axis, [(d, (d - have) % ways) for d in range(ways)])]
    slice x2, local copies, waits for them, and re-layouts: 9.24 us -> 3.32 us  [window_of(): field[:, first_row:first_row + row_count, first_col:first_col + column_co...]
  transfers between devices with their start and end apart: 11 -> 11, of which waited for: 9 -> 9; matrix products, arithmetic and copies ran while one was open for 6% -> 7% of each run, Pallas kernels for 0% -> 0%
where the time goes in v1:
time: 140 us; the launch traced here: 139 us
  waiting for transfers between devices  59.4 us (42%)
  blocking collectives  18.2 us (13%)
  between operations  15.9 us (11%)
  matrix products  15 us (11%)
  local copies, waits for them, and re-layouts  13.6 us (10%)
  starting transfers between devices  12.2 us (9%)
  other arithmetic  4.95 us (4%)
    psum x1, waiting for transfers between devices, local(): weight_grad, bias_grad = lax.psum((weight_part, bias_part), ('lon', 'lat'))  34 us
    psum x1, blocking collectives, local(): weight_grad, bias_grad = lax.psum((weight_part, bias_part), ('lon', 'lat'))  18.2 us
    ppermute x1, waiting for transfers between devices, doubled_up(): lax.ppermute(line, axis, [(d, (d - have) % ways) for d in range(ways)])  13.3 us
    reduce_scatter x1, waiting for transfers between devices, local(): lax.psum_scatter(summed.reshape(amount, row_count, column_count), 'chan',...  7.1 us
    unnamed x34, local copies, waits for them, and re-layouts  5.77 us
    dot_general x9, matrix products, local(): lax.dot_general(grad_pre, window, (((1,), (1,)), ((), ())), preferred_ele...  5.73 us
    ppermute x4, starting transfers between devices, padded_2(): after = lax.ppermute(initial, axis, down)  5.47 us
    dot_general x9, matrix products, local(): lax.dot_general(kernel_cols, window, (((0,), (0,)), ((), ())), preferred_...  5.08 us
  transfers between devices with their start and end apart: 11, of which 9 were waited for; matrix products, arithmetic and copies ran while one was open for 7% of the time, Pallas kernels for 0%

profile of v1, /device:TPU:0, one launch (start us, length us, event | category | flops | bytes accessed | tf_op | source)
XLA Modules:
  0.0 139.2 jit_solution(1489727267678419328)
XLA Ops:
  8.1 1.5 %copy.13 = bf16[128,16,128]{0,2,1:T(8,128)(2,1)S(1)} copy(bf16[128,16,128]{2,1,0:T(8,128)(2,1)} %param.4) | data formatting | bytes 1048576 | tf_op args[0]
  9.6 3.1 %collective-permute-start = (bf16[128,16,1]{0,2,1:T(2,128)(2,1)S(1)}, bf16[128,16,1]{0,2,1:T(2,128)(2,1)S(1)}, u32[]{:S(2)}, u32[]{:S(2)}) collective-permute-start(bf16[128,16,1]{0,2,1:T(2,128)(2,1)S(1)} %get-tuple-element.27), channel_id=1, source_target_pairs={{0,4},{4,8},{8,12},{12,0},{1,5},{5,9},{9,13},{13,1},{2,6},{6,10},{... | collective-permute-start | bytes 12296 | tf_op jit(solution)/shard_map/ppermute | solution.py:26
  12.7 2.1 %collective-permute-start.1 = (bf16[128,16,1]{0,2,1:T(2,128)(2,1)S(1)}, bf16[128,16,1]{0,2,1:T(2,128)(2,1)S(1)}, u32[]{:S(2)}, u32[]{:S(2)}) collective-permute-start(bf16[128,16,1]{0,2,1:T(2,128)(2,1)S(1)} %get-tuple-element.28), channel_id=1, source_target_pairs={{4,0},{8,4},{12,8},{0,12},{5,1},{9,5},{13,9},{1,13},{6,2},{10,6},{... | collective-permute-start | bytes 12296 | tf_op jit(solution)/shard_map/ppermute | solution.py:27
  14.8 1.6 %collective-permute-done = bf16[128,16,1]{0,2,1:T(2,128)(2,1)S(1)} collective-permute-done((bf16[128,16,1]{0,2,1:T(2,128)(2,1)S(1)}, bf16[128,16,1]{0,2,1:T(2,128)(2,1)S(1)}, u32[]{:S(2)}, u32[]{:S(2)}) %collective-permute-start) | collective-permute-done | bytes 4128 | tf_op jit(solution)/shard_map/ppermute | solution.py:26
  18.2 1.7 %collective-permute-start.4 = (bf16[128,18,130]{0,2,1:T(8,128)(2,1)S(1)}, bf16[128,18,130]{0,2,1:T(8,128)(2,1)S(1)}, u32[]{:S(2)}, u32[]{:S(2)}) collective-permute-start(bf16[128,18,130]{0,2,1:T(8,128)(2,1)S(1)} %maximum_select_fusion), channel_id=1, source_target_pairs={{0,2},{2,0},{1,3},{3,1},{4,6},{6,4},{5,7},{7,5},{8,10},{10,8},{9,1... | collective-permute-start | bytes 1797128 | tf_op jit(solution)/shard_map/ppermute | solution.py:12
  19.9 1.4 %copy.12 = f32[128,16,128]{0,2,1:T(8,128)} copy(bf16[128,16,128]{2,1,0:T(8,128)(2,1)S(1)} %copy-done.14) | data formatting | bytes 1572864 | tf_op jit(solution)/shard_map/convert_element_type | solution.py:66
  21.3 13.3 %collective-permute-done.4 = bf16[128,18,130]{0,2,1:T(8,128)(2,1)S(1)} collective-permute-done((bf16[128,18,130]{0,2,1:T(8,128)(2,1)S(1)}, bf16[128,18,130]{0,2,1:T(8,128)(2,1)S(1)}, u32[]{:S(2)}, u32[]{:S(2)}) %collective-permute-start.4) | collective-permute-done | bytes 599072 | tf_op jit(solution)/shard_map/ppermute | solution.py:12
  34.6 1.0 fusion.4
  35.6 2.4 %fusion.49 = (bf16[256,16,128]{0,2,1:T(8,128)(2,1)S(1)}, bf16[256,16,128]{0,2,1:T(8,128)(2,1)S(1)}, bf16[256,16,128]{0,2,1:T(8,128)(2,1)S(1)}, bf16[256,16,128]{...) fusion(bf16[256,18,130]{0,2,1:T(8,128)(2,1)S(1)} %fusion.4), kind=kLoop, calls=%fused_computation.93 | loop fusion | bytes 18874368 | tf_op jit(solution)/shard_map/slice | solution.py:49
  41.7 0.8 copy-done.13
  43.3 1.5 %collective-permute-start.5 = (bf16[128,16,1]{0,2,1:T(2,128)(2,1)S(1)}, bf16[128,16,1]{0,2,1:T(2,128)(2,1)S(1)}, u32[]{:S(2)}, u32[]{:S(2)}) collective-permute-start(bf16[128,16,1]{0,2,1:T(2,128)(2,1)S(1)} %get-tuple-element.25), channel_id=1, source_target_pairs={{0,4},{4,8},{8,12},{12,0},{1,5},{5,9},{9,13},{13,1},{2,6},{6,10},{... | collective-permute-start | bytes 12296 | tf_op jit(solution)/shard_map/ppermute | solution.py:26
  44.8 2.4 %collective-permute-start.6 = (bf16[128,16,1]{0,2,1:T(2,128)(2,1)S(1)}, bf16[128,16,1]{0,2,1:T(2,128)(2,1)S(1)}, u32[]{:S(2)}, u32[]{:S(2)}) collective-permute-start(bf16[128,16,1]{0,2,1:T(2,128)(2,1)S(1)} %get-tuple-element.26), channel_id=1, source_target_pairs={{4,0},{8,4},{12,8},{0,12},{5,1},{9,5},{13,9},{1,13},{6,2},{10,6},{... | collective-permute-start | bytes 12296 | tf_op jit(solution)/shard_map/ppermute | solution.py:27
  47.2 1.6 %collective-permute-done.5 = bf16[128,16,1]{0,2,1:T(2,128)(2,1)S(1)} collective-permute-done((bf16[128,16,1]{0,2,1:T(2,128)(2,1)S(1)}, bf16[128,16,1]{0,2,1:T(2,128)(2,1)S(1)}, u32[]{:S(2)}, u32[]{:S(2)}) %collective-permute-start.5) | collective-permute-done | bytes 4128 | tf_op jit(solution)/shard_map/ppermute | solution.py:26
  50.6 0.9 fusion.50
  54.9 1.7 %convolution_add_fusion = f32[2048,256]{1,0:T(8,128)} fusion(f32[2048,256]{1,0:T(8,128)S(1)} %convolution_add_fusion.1, bf16[128,2048]{0,1:T(8,128)(2,1)S(1)} %bitcast.157, bf16[3,3,128,256]{3,2,1,0:T(8,128)(2,1)S(1)} %copy-done.12), kind=kOutput, calls=%fused_computation | convolution fusion | flops 134742016 | bytes 4784128 | tf_op jit(solution)/shard_map/dot_general | solution.py:90
  56.6 3.0 %copy.16 = f32[256,16,128]{2,1,0:T(8,128)} copy(f32[256,16,128]{0,2,1:T(8,128)} %bitcast.154) | data formatting | bytes 4194304 | tf_op jit(solution)/shard_map/reshape | solution.py:94
  59.9 1.7 %convolution_bitcast_fusion = f32[1,128,256]{2,1,0:T(8,128)S(1)} fusion(bf16[128,2048]{0,1:T(8,128)(2,1)S(1)} %get-tuple-element.30, bf16[256,2048]{0,1:T(8,128)(2,1)} %bitcast.156), kind=kOutput, calls=%fused_computation.27 | convolution fusion | flops 134217728 | bytes 1703936 | tf_op jit(solution)/shard_map/dot_general | solution.py:75
  61.6 1.7 %convolution_bitcast_fusion.1 = f32[1,128,256]{2,1,0:T(8,128)S(1)} fusion(bf16[128,2048]{0,1:T(8,128)(2,1)S(1)} %get-tuple-element.30, bf16[256,2048]{0,1:T(8,128)(2,1)} %bitcast.153), kind=kOutput, calls=%fused_computation.28 | convolution fusion | flops 134217728 | bytes 1703936 | tf_op jit(solution)/shard_map/dot_general | solution.py:75
  66.9 1.1 pad_maximum_fusion
  68.0 18.2 %psum.15 = f32[128]{0:T(128)} all-reduce(f32[128]{0:T(128)S(1)} %get-tuple-element.29), channel_id=1, replica_groups=mesh['groups'=2,'lon'=4,'chan'=2,'lat'=2] {'lon','lat'}, use_global_device_ids=true, to_apply=%region_3.4 | all-reduce | flops 128 | bytes 1024 | tf_op jit(solution)/shard_map/psum | solution.py:81
  86.2 7.1 %reduce-scatter.2.cloned.1.call-done = f32[128,16,128]{2,1,0:T(8,128)} async-done(((f32[256,16,128]{2,1,0:T(8,128)}), f32[128,16,128]{2,1,0:T(8,128)}) %reduce-scatter.2.cloned.1.call-update) | async-done | bytes 1048592 | tf_op jit(solution)/shard_map/reduce_scatter | solution.py:93
  93.3 2.1 %convert_element_type.18 = bf16[128,16,128]{2,1,0:T(8,128)(2,1)} convert(f32[128,16,128]{2,1,0:T(8,128)} %reduce-scatter.2.cloned.1.call-done) | non-fusion elementwise | flops 262144 | bytes 1572864 | tf_op jit(solution)/shard_map/convert_element_type | solution.py:96
  95.4 34.0 %all-reduce.2.cloned.1.call-done = f32[3,3,128,256]{3,2,1,0:T(8,128)} async-done(((f32[3,3,128,256]{3,2,1,0:T(8,128)}), f32[3,3,128,256]{3,2,1,0:T(8,128)}) %all-reduce.2.cloned.1.call-update) | async-done | bytes 1179664 | tf_op jit(solution)/shard_map/psum | solution.py:81
  129.4 2.4 %copy.18 = f32[3,3,128,256]{3,2,1,0:T(8,128)} copy(f32[3,3,128,256]{3,2,1,0:T(8,128)} %all-reduce.2.cloned.1.call-done) | data formatting | bytes 2359296
  (78 shorter events, 15.1 us)
Async XLA Ops:
  8.0 11.9 %copy-start.14 = (bf16[128,16,128]{2,1,0:T(8,128)(2,1)S(1)}, bf16[128,16,128]{2,1,0:T(8,128)(2,1)}, u32[]{:S(2)}) copy-start(bf16[128,16,128]{2,1,0:T(8,128)(2,1)} %param.5) | copy-start | bytes 1572868
  8.0 85.3 %reduce-scatter.2.cloned.1.call-start = ((), (), s32[]{:S(2)}) async-start(), calls=%async_computation.1 | async-start | bytes 3145728 | tf_op jit(solution)/shard_map/reduce_scatter | solution.py:93
  9.6 6.8 %collective-permute-start = (bf16[128,16,1]{0,2,1:T(2,128)(2,1)S(1)}, bf16[128,16,1]{0,2,1:T(2,128)(2,1)S(1)}, u32[]{:S(2)}, u32[]{:S(2)}) collective-permute-start(bf16[128,16,1]{0,2,1:T(2,128)(2,1)S(1)} %get-tuple-element.27), channel_id=1, source_target_pairs={{0,4},{4,8},{8,12},{12,0},{1,5},{5,9},{9,13},{13,1},{2,6},{6,10},{... | collective-permute-start | bytes 12296 | tf_op jit(solution)/shard_map/ppermute | solution.py:26
  12.7 3.7 %collective-permute-start.1 = (bf16[128,16,1]{0,2,1:T(2,128)(2,1)S(1)}, bf16[128,16,1]{0,2,1:T(2,128)(2,1)S(1)}, u32[]{:S(2)}, u32[]{:S(2)}) collective-permute-start(bf16[128,16,1]{0,2,1:T(2,128)(2,1)S(1)} %get-tuple-element.28), channel_id=1, source_target_pairs={{4,0},{8,4},{12,8},{0,12},{5,1},{9,5},{13,9},{1,13},{6,2},{10,6},{... | collective-permute-start | bytes 12296 | tf_op jit(solution)/shard_map/ppermute | solution.py:27
  16.4 1.3 collective-permute-start.2
  16.5 1.4 collective-permute-start.3
  18.2 16.4 %collective-permute-start.4 = (bf16[128,18,130]{0,2,1:T(8,128)(2,1)S(1)}, bf16[128,18,130]{0,2,1:T(8,128)(2,1)S(1)}, u32[]{:S(2)}, u32[]{:S(2)}) collective-permute-start(bf16[128,18,130]{0,2,1:T(8,128)(2,1)S(1)} %maximum_select_fusion), channel_id=1, source_target_pairs={{0,2},{2,0},{1,3},{3,1},{4,6},{6,4},{5,7},{7,5},{8,10},{10,8},{9,1... | collective-permute-start | bytes 1797128 | tf_op jit(solution)/shard_map/ppermute | solution.py:12
  35.6 2.5 %copy-start.12 = (bf16[3,3,128,256]{3,2,1,0:T(8,128)(2,1)S(1)}, bf16[3,3,128,256]{3,2,1,0:T(8,128)(2,1)}, u32[]{:S(2)}) copy-start(bf16[3,3,128,256]{3,2,1,0:T(8,128)(2,1)} %param.6) | copy-start | bytes 1769476
  38.1 1.4 %copy-start.2 = (bf16[256,16,128]{0,2,1:T(8,128)(2,1)}, bf16[256,16,128]{0,2,1:T(8,128)(2,1)S(1)}, u32[]{:S(2)}) copy-start(bf16[256,16,128]{0,2,1:T(8,128)(2,1)S(1)} %get-tuple-element.8) | copy-start | bytes 3145732
  38.1 1.9 %copy-start.4 = (bf16[256,16,128]{0,2,1:T(8,128)(2,1)}, bf16[256,16,128]{0,2,1:T(8,128)(2,1)S(1)}, u32[]{:S(2)}) copy-start(bf16[256,16,128]{0,2,1:T(8,128)(2,1)S(1)} %get-tuple-element.7) | copy-start | bytes 3145732
  38.1 2.3 %copy-start.6 = (bf16[256,16,128]{0,2,1:T(8,128)(2,1)}, bf16[256,16,128]{0,2,1:T(8,128)(2,1)S(1)}, u32[]{:S(2)}) copy-start(bf16[256,16,128]{0,2,1:T(8,128)(2,1)S(1)} %get-tuple-element.6) | copy-start | bytes 3145732
  38.1 2.7 %copy-start.8 = (bf16[256,16,128]{0,2,1:T(8,128)(2,1)}, bf16[256,16,128]{0,2,1:T(8,128)(2,1)S(1)}, u32[]{:S(2)}) copy-start(bf16[256,16,128]{0,2,1:T(8,128)(2,1)S(1)} %get-tuple-element.5) | copy-start | bytes 3145732
  38.1 3.2 %copy-start.10 = (bf16[256,16,128]{0,2,1:T(8,128)(2,1)}, bf16[256,16,128]{0,2,1:T(8,128)(2,1)S(1)}, u32[]{:S(2)}) copy-start(bf16[256,16,128]{0,2,1:T(8,128)(2,1)S(1)} %get-tuple-element.4) | copy-start | bytes 3145732
  38.1 3.6 %copy-start.11 = (bf16[256,16,128]{0,2,1:T(8,128)(2,1)}, bf16[256,16,128]{0,2,1:T(8,128)(2,1)S(1)}, u32[]{:S(2)}) copy-start(bf16[256,16,128]{0,2,1:T(8,128)(2,1)S(1)} %get-tuple-element.3) | copy-start | bytes 3145732
  41.3 1.2 copy-start.13
  43.3 5.5 %collective-permute-start.5 = (bf16[128,16,1]{0,2,1:T(2,128)(2,1)S(1)}, bf16[128,16,1]{0,2,1:T(2,128)(2,1)S(1)}, u32[]{:S(2)}, u32[]{:S(2)}) collective-permute-start(bf16[128,16,1]{0,2,1:T(2,128)(2,1)S(1)} %get-tuple-element.25), channel_id=1, source_target_pairs={{0,4},{4,8},{8,12},{12,0},{1,5},{5,9},{9,13},{13,1},{2,6},{6,10},{... | collective-permute-start | bytes 12296 | tf_op jit(solution)/shard_map/ppermute | solution.py:26
  44.8 4.0 %collective-permute-start.6 = (bf16[128,16,1]{0,2,1:T(2,128)(2,1)S(1)}, bf16[128,16,1]{0,2,1:T(2,128)(2,1)S(1)}, u32[]{:S(2)}, u32[]{:S(2)}) collective-permute-start(bf16[128,16,1]{0,2,1:T(2,128)(2,1)S(1)} %get-tuple-element.26), channel_id=1, source_target_pairs={{4,0},{8,4},{12,8},{0,12},{5,1},{9,5},{13,9},{1,13},{6,2},{10,6},{... | collective-permute-start | bytes 12296 | tf_op jit(solution)/shard_map/ppermute | solution.py:27
  48.8 1.3 collective-permute-start.7
  48.9 1.4 collective-permute-start.8
  59.7 69.7 %all-reduce.2.cloned.1.call-start = ((), (), s32[]{:S(2)}) async-start(), calls=%async_computation.2 | async-start | bytes 2359296 | tf_op jit(solution)/shard_map/psum | solution.py:81
  59.9 3.3 %copy-start.9 = (bf16[256,16,128]{0,2,1:T(8,128)(2,1)S(1)}, bf16[256,16,128]{0,2,1:T(8,128)(2,1)}, u32[]{:S(2)}) copy-start(bf16[256,16,128]{0,2,1:T(8,128)(2,1)} %copy-done.8) | copy-start | bytes 3145732
  61.6 2.1 %copy-start.7 = (bf16[256,16,128]{0,2,1:T(8,128)(2,1)S(1)}, bf16[256,16,128]{0,2,1:T(8,128)(2,1)}, u32[]{:S(2)}) copy-start(bf16[256,16,128]{0,2,1:T(8,128)(2,1)} %copy-done.6) | copy-start | bytes 3145732
  63.6 1.3 copy-start.3
  64.5 1.3 copy-start.1
  (3 other events, 3.4 us)
Sparse Core Ops, SparseCore 0:
  59.8 33.4 reduce-scatter.1
Sparse Core Ops, SparseCore 1:
  68.1 61.2 all-reduce.1
